TPU v7x, 32 devices: a whole 2x2x4 slice. The times are simulated.
32 devices in a mesh: dp: 2 (over core), expert: 16 (over z, y, x).
Axes of the slice: x: 2, y: 2, z: 4, core: 2. Of those that a mesh axis runs over, the one named last changes fastest.
Arguments:
- tokens: bfloat16 [1024, 3584], P(('dp', 'expert')), may hold values from -6 to 6
- out_grad: bfloat16 [1024, 3584], P(('dp', 'expert')), may hold values from -6 to 6
- expert_ids: int32 [1024, 8], P(('dp', 'expert')), may hold values from 0 to 15, all different within a row; in each aligned block of 32 rows (0 to 31, 32 to 63, ...) at most 20 rows name the same one
- gate_probs: float32 [1024, 8], P(('dp', 'expert')), may hold values from 0.2 to 1.5
- weights: bfloat16 [16, 3584, 3, 128], P('expert', 'dp'), may hold values from -0.09375 to 0.09375
- first_moment: bfloat16 [16, 3584, 3, 128], P('expert', 'dp'), may hold values from -6 to 6
- second_moment: bfloat16 [16, 3584, 3, 128], P('expert', 'dp'), may hold values from 0.5 to 5
- moving_pairs: int32 [8], replicated, may hold values from 0 to 1, as said below
Outputs:
- token_grad: bfloat16 [1024, 3584], P(('dp', 'expert'))
- prob_grad: bfloat16 [1024, 8], P(('dp', 'expert'))
- moved_weights: bfloat16 [16, 3584, 3, 128], P('expert', 'dp')
- weight_grad: float32 [16, 3584, 3, 128], P('expert', 'dp')
- new_first: bfloat16 [16, 3584, 3, 128], P('expert', 'dp')
- new_second: bfloat16 [16, 3584, 3, 128], P('expert', 'dp')
Inputs may be any that keep to these rules, and one draw needn't show every extreme that they name: `expert_ids`: each row names 8 different experts. Among the entries of the 32 rows of one device, no expert is named more than 20 times, a bound that some block reaches. `moving_pairs`: entry p is 1 where devices p and p + 8 of the expert axis exchange their experts. The last entry is always 1.
All inputs are finite; a program needn't handle non-finite values.
Results may differ from a plain program's by a relative error of at most 0.018.
Values may be sent and summed in bfloat16 or wider, within the bound.
No kernel may reach another device: no remote copies, remote signals or barrier semaphores. Data moves between devices by JAX's collectives and lax.ppermute only.
A program may use at most 64 MiB of HBM per device.

v0:
```python
import jax
import jax.numpy as jnp
from jax import lax
from jax.sharding import PartitionSpec as P


def from_partner(value, axis, bit):
    return lax.ppermute(value, axis, [(i, i ^ 1 << bit) for i in range(lax.axis_size(axis))])


def silu_parts(pre_gate):
    sig = jax.nn.sigmoid(pre_gate)
    return (pre_gate * sig, sig * (1.0 + pre_gate * (1.0 - sig)))


def on_device(
    tokens, out_grad, expert_ids, gate_probs, weights, first_moment, second_moment, moving_pairs
):
    axis_width = lax.axis_size("expert")
    half_axis = axis_width // 2
    swap_bit = half_axis.bit_length() - 1
    groups = lax.axis_size("dp")
    my_index = lax.axis_index("expert")
    tok_rows, route_count = expert_ids.shape
    model_width = tokens.shape[1]
    entry_count = tok_rows * route_count
    slot_cap = 5 * entry_count // (4 * axis_width)
    slot_count = axis_width * slot_cap
    pair_lanes = jnp.arange(half_axis, dtype=jnp.int32)
    my_move = jnp.sum(jnp.where(pair_lanes == my_index % half_axis, moving_pairs, 0))
    swapped = my_move == 1
    flat_ids = expert_ids.reshape(-1)
    theirs = from_partner((weights, first_moment, second_moment), "expert", swap_bit)
    weights = jnp.where(swapped, theirs[0], weights)
    first_moment = jnp.where(swapped, theirs[1], first_moment)
    second_moment = jnp.where(swapped, theirs[2], second_moment)
    lane_hit = (flat_ids % half_axis)[:, None] == pair_lanes[None, :]
    moves = jnp.sum(jnp.where(lane_hit, moving_pairs[None, :], 0), axis=1)
    target_dev = jnp.where(moves == 1, (flat_ids + half_axis) % axis_width, flat_ids)
    id_onehot = (flat_ids[:, None] == jnp.arange(axis_width, dtype=jnp.int32)[None, :]).astype(
        jnp.int32
    )
    id_rank = jnp.sum((jnp.cumsum(id_onehot, axis=0) - id_onehot) * id_onehot, axis=1)
    slot_of = target_dev * slot_cap + id_rank
    slot_hit = jnp.arange(slot_count, dtype=jnp.int32)[:, None] == slot_of[None, :]
    filled = jnp.any(slot_hit, axis=1)
    entry_lanes = jnp.arange(entry_count, dtype=jnp.int32)
    slot_entry = jnp.sum(jnp.where(slot_hit, entry_lanes[None, :], 0), axis=1)
    token_of = slot_entry // route_count
    flat_gate = gate_probs.reshape(-1)
    zero_row = jnp.zeros((), jnp.bfloat16)
    send_rows = jnp.where(filled[:, None], tokens[token_of], zero_row).reshape(
        axis_width, slot_cap, model_width
    )
    send_grads = jnp.where(filled[:, None], out_grad[token_of], zero_row).reshape(
        axis_width, slot_cap, model_width
    )
    send_gate = (
        jnp.where(filled, flat_gate[slot_entry], 0.0)
        .astype(jnp.bfloat16)
        .reshape(axis_width, slot_cap)
    )
    recv_rows, recv_grads, recv_gate = (
        lax.all_to_all(send_rows, "expert", split_axis=0, concat_axis=0, tiled=True),
        lax.all_to_all(send_grads, "expert", split_axis=0, concat_axis=0, tiled=True),
        lax.all_to_all(send_gate, "expert", split_axis=0, concat_axis=0, tiled=True),
    )
    whole = lax.all_gather(weights, "dp", axis=1, tiled=True)[0]
    w_gate = whole[:, 0, :]
    w_up = whole[:, 1, :]
    w_down = whole[:, 2, :]
    w_both = jnp.concatenate([w_gate, w_up], axis=1)
    rows = recv_rows.reshape(slot_count, model_width)
    pre_gate = jnp.dot(rows, w_gate, preferred_element_type=jnp.float32)
    pre_up = jnp.dot(rows, w_up, preferred_element_type=jnp.float32)
    activated, act_slope = silu_parts(pre_gate)
    hidden = (activated * pre_up).astype(jnp.bfloat16)
    contract_hidden = (((1,), (1,)), ((), ()))
    grads_in = recv_grads.reshape(slot_count, model_width)
    gates = recv_gate.reshape(slot_count).astype(jnp.float32)
    projected = jnp.dot(grads_in, w_down, preferred_element_type=jnp.float32)
    gate_rows = jnp.sum(hidden.astype(jnp.float32) * projected, axis=1).astype(jnp.bfloat16)
    scaled_grad = (gates[:, None] * grads_in.astype(jnp.float32)).astype(jnp.bfloat16)
    hidden_grad = jnp.dot(scaled_grad, w_down, preferred_element_type=jnp.float32)
    gate_delta = (hidden_grad * pre_up * act_slope).astype(jnp.bfloat16)
    up_delta = (hidden_grad * activated).astype(jnp.bfloat16)
    both_delta = jnp.concatenate([gate_delta, up_delta], axis=1)
    row_grad = lax.dot_general(
        both_delta, w_both, contract_hidden, preferred_element_type=jnp.float32
    )
    row_grad = row_grad.astype(jnp.bfloat16)
    back_rows, back_gate = (
        lax.all_to_all(
            row_grad.reshape(axis_width, slot_cap, model_width),
            "expert",
            split_axis=0,
            concat_axis=0,
            tiled=True,
        ),
        lax.all_to_all(
            gate_rows.reshape(axis_width, slot_cap),
            "expert",
            split_axis=0,
            concat_axis=0,
            tiled=True,
        ),
    )
    contract_rows = (((0,), (0,)), ((), ()))
    grad_gate = lax.dot_general(rows, gate_delta, contract_rows, preferred_element_type=jnp.float32)
    grad_up = lax.dot_general(rows, up_delta, contract_rows, preferred_element_type=jnp.float32)
    grad_down = lax.dot_general(
        scaled_grad, hidden, contract_rows, preferred_element_type=jnp.float32
    )
    grad = lax.psum_scatter(
        jnp.stack([grad_gate, grad_up, grad_down], axis=1).astype(jnp.bfloat16),
        "dp",
        scatter_dimension=0,
        tiled=True,
    ).astype(jnp.float32) * (1.0 / groups)
    grad = grad[None]
    new_first = (0.9 * first_moment.astype(jnp.float32) + 0.1 * grad).astype(jnp.bfloat16)
    new_second = (0.95 * second_moment.astype(jnp.float32) + 0.05 * grad * grad).astype(
        jnp.bfloat16
    )
    gathered = back_rows.reshape(slot_count, model_width)[slot_of].astype(jnp.float32)
    token_grad = (
        (gathered * flat_gate[:, None])
        .reshape(tok_rows, route_count, model_width)
        .sum(axis=1)
        .astype(jnp.bfloat16)
    )
    prob_grad = back_gate.reshape(slot_count)[slot_of].reshape(tok_rows, route_count)
    return (token_grad, prob_grad, weights, grad, new_first, new_second)


def solution(mesh):
    in_specs = (
        P(("dp", "expert"), None),
        P(("dp", "expert"), None),
        P(("dp", "expert"), None),
        P(("dp", "expert"), None),
        P("expert", "dp", None, None),
        P("expert", "dp", None, None),
        P("expert", "dp", None, None),
        P(),
    )
    out_specs = (
        P(("dp", "expert"), None),
        P(("dp", "expert"), None),
        P("expert", "dp", None, None),
        P("expert", "dp", None, None),
        P("expert", "dp", None, None),
        P("expert", "dp", None, None),
    )
    return jax.shard_map(
        on_device, mesh=mesh, in_specs=in_specs, out_specs=out_specs, check_vma=False
    )
```

profile of v0, /device:TPU:0, one launch (start us, length us, event | category | flops | bytes accessed | tf_op | source)
XLA Modules:
  0.0 456.9 jit_solution(9229121527226329171)
XLA Ops:
  14.1 8.3 %all-to-all-start = ((bf16[16,1,20]{2,1,0:T(2,128)(2,1)}), bf16[16,1,20]{2,1,0:T(2,128)(2,1)S(1)}, u32[]{:S(2)}, u32[]{:S(2)}) async-start(bf16[16,1,20]{2,1,0:T(2,128)(2,1)} %convert_element_type.137), calls=%async_computation | async-start | bytes 16384 | tf_op jit(solution)/shard_map/all_to_all | solution.py:66
  22.6 3.7 gather_fusion.1
  28.9 3.7 gather_fusion.2
  32.6 4.1 gather.23
  36.7 4.7 %broadcast_select_fusion = (bf16[16,20,3584]{2,1,0:T(8,128)(2,1)}, bf16[16,20,3584]{2,1,0:T(8,128)(2,1)}) fusion(bf16[16,20,3584]{2,1,0:T(8,128)(2,1)} %gather.23, pred[16,20]{1,0:T(8,128)(4,1)S(1)} %broadcast_in_dim.73, bf16[16,20,3584]{2,1,0:T(8,128)(2,1)S(1)} %gather.21), kind=kLoop, calls=%fused_computation.28 | loop fusion | flops 2293760 | bytes 9175360 | tf_op jit(solution)/shard_map/jit(_where)/select_n | solution.py:52
  41.4 6.9 %all-to-all-start.1 = ((bf16[16,20,3584]{2,1,0:T(8,128)(2,1)}), bf16[16,20,3584]{2,1,0:T(8,128)(2,1)S(1)}, u32[]{:S(2)}, u32[]{:S(2)}) async-start(bf16[16,20,3584]{2,1,0:T(8,128)(2,1)} %get-tuple-element.42), calls=%async_computation.1 | async-start | bytes 5505024 | tf_op jit(solution)/shard_map/all_to_all | solution.py:65
  48.3 2.8 collective-permute-start
  51.2 80.3 %all-to-all-done.1 = bf16[16,20,3584]{2,1,0:T(8,128)(2,1)S(1)} async-done(((bf16[16,20,3584]{2,1,0:T(8,128)(2,1)}), bf16[16,20,3584]{2,1,0:T(8,128)(2,1)S(1)}, u32[]{:S(2)}, u32[]{:S(2)}) %all-to-all-start.1) | async-done | bytes 2293792 | tf_op jit(solution)/shard_map/all_to_all | solution.py:65
  131.5 14.8 %all-to-all-start.2 = ((bf16[16,20,3584]{2,1,0:T(8,128)(2,1)}), bf16[16,20,3584]{2,1,0:T(8,128)(2,1)}, u32[]{:S(2)}, u32[]{:S(2)}) async-start(bf16[16,20,3584]{2,1,0:T(8,128)(2,1)} %get-tuple-element.41), calls=%async_computation.2 | async-start | bytes 5505024 | tf_op jit(solution)/shard_map/all_to_all | solution.py:64
  147.7 52.0 %collective-permute-done = bf16[1,1792,3,128]{3,1,2,0:T(8,128)(2,1)} collective-permute-done((bf16[1,1792,3,128]{3,1,2,0:T(8,128)(2,1)}, bf16[1,1792,3,128]{3,1,2,0:T(8,128)(2,1)}, u32[]{:S(2)}, u32[]{:S(2)}) %collective-permute-start) | collective-permute-done | bytes 1376288 | tf_op jit(solution)/shard_map/ppermute | solution.py:8
  207.8 6.0 %all-gather.2.cloned.1.call-done = bf16[1,3584,3,128]{3,1,2,0:T(8,128)(2,1)} async-done(((bf16[1,1792,3,128]{3,1,2,0:T(8,128)(2,1)}), bf16[1,3584,3,128]{3,1,2,0:T(8,128)(2,1)}) %all-gather.2.cloned.1.call-update) | async-done | bytes 2752528 | tf_op jit(solution)/shard_map/all_gather | solution.py:68
  215.8 4.3 all-to-all-done.2
  220.1 2.7 reshape.344
  242.1 12.8 %all-to-all-start.4 = ((bf16[16,1,20]{2,1,0:T(2,128)(2,1)}), bf16[16,1,20]{2,1,0:T(2,128)(2,1)S(1)}, u32[]{:S(2)}, u32[]{:S(2)}) async-start(bf16[16,1,20]{2,1,0:T(2,128)(2,1)} %convert_element_type.138), calls=%async_computation.4 | async-start | bytes 16384 | tf_op jit(solution)/shard_map/all_to_all | solution.py:100
  259.1 3.0 all-to-all-done.4
  262.1 4.7 %all-to-all-start.3 = ((bf16[16,20,3584]{2,1,0:T(8,128)(2,1)}), bf16[16,20,3584]{2,1,0:T(8,128)(2,1)}, u32[]{:S(2)}, u32[]{:S(2)}) async-start(bf16[16,20,3584]{2,1,0:T(8,128)(2,1)} %reshape.345), calls=%async_computation.3 | async-start | bytes 5505024 | tf_op jit(solution)/shard_map/all_to_all | solution.py:93
  272.8 105.2 %all-to-all-done.3 = bf16[16,20,3584]{2,1,0:T(8,128)(2,1)} async-done(((bf16[16,20,3584]{2,1,0:T(8,128)(2,1)}), bf16[16,20,3584]{2,1,0:T(8,128)(2,1)}, u32[]{:S(2)}, u32[]{:S(2)}) %all-to-all-start.3) | async-done | bytes 2293792 | tf_op jit(solution)/shard_map/all_to_all | solution.py:93
  378.0 2.7 reshape.346
  380.7 2.9 gather_fusion.3
  383.7 3.6 fusion.3
  387.3 3.2 fusion.5
  390.5 26.3 %collective-permute-done.1 = bf16[1,1792,3,128]{3,1,2,0:T(8,128)(2,1)} collective-permute-done((bf16[1,1792,3,128]{3,1,2,0:T(8,128)(2,1)}, bf16[1,1792,3,128]{3,1,2,0:T(8,128)(2,1)}, u32[]{:S(2)}, u32[]{:S(2)}) %collective-permute-start.1) | collective-permute-done | bytes 1376288 | tf_op jit(solution)/shard_map/ppermute | solution.py:8
  416.8 28.4 %collective-permute-done.2 = bf16[1,1792,3,128]{3,1,2,0:T(8,128)(2,1)} collective-permute-done((bf16[1,1792,3,128]{3,1,2,0:T(8,128)(2,1)}, bf16[1,1792,3,128]{3,1,2,0:T(8,128)(2,1)}, u32[]{:S(2)}, u32[]{:S(2)}) %collective-permute-start.2) | collective-permute-done | bytes 1376288 | tf_op jit(solution)/shard_map/ppermute | solution.py:8
  445.3 4.8 %fusion.8 = (bf16[1,1792,3,128]{3,1,2,0:T(8,128)(2,1)}, bf16[1,1792,3,128]{3,1,2,0:T(8,128)(2,1)}) fusion(bf16[1792,3,128]{2,0,1:T(8,128)(2,1)S(1)} %copy-done.4, bf16[1,1792,3,128]{3,1,2,0:T(8,128)(2,1)} %collective-permute-done.2, bf16[1,1792,3,128]{3,1,2,0:T(8,128)(2,1)} %param.14, pred[]{:T(512)S(6)} %eq.100, ...), kind=kLoop, calls=%fused_computation.23 | loop fusion | flops 10321920 | bytes 9633793 | tf_op jit(solution)/shard_map/convert_element_type | solution.py:122
  (75 shorter events, 49.7 us)
Async XLA Ops:
  7.2 15.4 %copy-start = (bf16[32,3584]{1,0:T(8,128)(2,1)S(1)}, bf16[32,3584]{1,0:T(8,128)(2,1)}, u32[]{:S(2)}) copy-start(bf16[32,3584]{1,0:T(8,128)(2,1)} %param.9) | copy-start | bytes 688132
  14.1 27.3 %all-to-all-start = ((bf16[16,1,20]{2,1,0:T(2,128)(2,1)}), bf16[16,1,20]{2,1,0:T(2,128)(2,1)S(1)}, u32[]{:S(2)}, u32[]{:S(2)}) async-start(bf16[16,1,20]{2,1,0:T(2,128)(2,1)} %convert_element_type.137), calls=%async_computation | async-start | bytes 16384 | tf_op jit(solution)/shard_map/all_to_all | solution.py:66
  26.3 2.6 copy-start.2
  41.4 90.0 %all-to-all-start.1 = ((bf16[16,20,3584]{2,1,0:T(8,128)(2,1)}), bf16[16,20,3584]{2,1,0:T(8,128)(2,1)S(1)}, u32[]{:S(2)}, u32[]{:S(2)}) async-start(bf16[16,20,3584]{2,1,0:T(8,128)(2,1)} %get-tuple-element.42), calls=%async_computation.1 | async-start | bytes 5505024 | tf_op jit(solution)/shard_map/all_to_all | solution.py:65
  48.3 151.4 %collective-permute-start = (bf16[1,1792,3,128]{3,1,2,0:T(8,128)(2,1)}, bf16[1,1792,3,128]{3,1,2,0:T(8,128)(2,1)}, u32[]{:S(2)}, u32[]{:S(2)}) collective-permute-start(bf16[1,1792,3,128]{3,1,2,0:T(8,128)(2,1)} %param.12), channel_id=1, source_target_pairs={{0,8},{1,9},{2,10},{3,11},{4,12},{5,13},{6,14},{7,15},{8,0},{9,1},... | collective-permute-start | bytes 4128776 | tf_op jit(solution)/shard_map/ppermute | solution.py:8
  131.5 71.2 %copy-start.3 = (bf16[16,20,3584]{2,1,0:T(8,128)(2,1)}, bf16[16,20,3584]{2,1,0:T(8,128)(2,1)S(1)}, u32[]{:S(2)}) copy-start(bf16[16,20,3584]{2,1,0:T(8,128)(2,1)S(1)} %all-to-all-done.1) | copy-start | bytes 6881284
  131.5 14.9 %copy-start.6 = (s32[8]{0:T(128)S(1)}, s32[8]{0:T(128)}, u32[]{:S(2)}) copy-start(s32[8]{0:T(128)} %param.15) | copy-start | bytes 100
  131.5 88.6 %all-to-all-start.2 = ((bf16[16,20,3584]{2,1,0:T(8,128)(2,1)}), bf16[16,20,3584]{2,1,0:T(8,128)(2,1)}, u32[]{:S(2)}, u32[]{:S(2)}) async-start(bf16[16,20,3584]{2,1,0:T(8,128)(2,1)} %get-tuple-element.41), calls=%async_computation.2 | async-start | bytes 5505024 | tf_op jit(solution)/shard_map/all_to_all | solution.py:64
  146.3 67.5 %all-gather.2.cloned.1.call-start = ((), (), s32[]{:S(2)}) async-start(), calls=%async_computation.6 | async-start | bytes 4128768 | tf_op jit(solution)/shard_map/all_gather | solution.py:68
  202.3 185.1 %reduce-scatter.2.cloned.1.call-start = ((), (), s32[]{:S(2)}) async-start(), calls=%async_computation.7 | async-start | bytes 4128768 | tf_op jit(solution)/shard_map/reduce_scatter | solution.py:114
  232.9 2.1 copy-start.5
  236.8 2.5 copy-start.7
  242.1 20.0 %all-to-all-start.4 = ((bf16[16,1,20]{2,1,0:T(2,128)(2,1)}), bf16[16,1,20]{2,1,0:T(2,128)(2,1)S(1)}, u32[]{:S(2)}, u32[]{:S(2)}) async-start(bf16[16,1,20]{2,1,0:T(2,128)(2,1)} %convert_element_type.138), calls=%async_computation.4 | async-start | bytes 16384 | tf_op jit(solution)/shard_map/all_to_all | solution.py:100
  262.1 115.9 %all-to-all-start.3 = ((bf16[16,20,3584]{2,1,0:T(8,128)(2,1)}), bf16[16,20,3584]{2,1,0:T(8,128)(2,1)}, u32[]{:S(2)}, u32[]{:S(2)}) async-start(bf16[16,20,3584]{2,1,0:T(8,128)(2,1)} %reshape.345), calls=%async_computation.3 | async-start | bytes 5505024 | tf_op jit(solution)/shard_map/all_to_all | solution.py:93
  266.8 150.0 %collective-permute-start.1 = (bf16[1,1792,3,128]{3,1,2,0:T(8,128)(2,1)}, bf16[1,1792,3,128]{3,1,2,0:T(8,128)(2,1)}, u32[]{:S(2)}, u32[]{:S(2)}) collective-permute-start(bf16[1,1792,3,128]{3,1,2,0:T(8,128)(2,1)} %param.13), channel_id=1, source_target_pairs={{0,8},{1,9},{2,10},{3,11},{4,12},{5,13},{6,14},{7,15},{8,0},{9,1},... | collective-permute-start | bytes 4128776 | tf_op jit(solution)/shard_map/ppermute | solution.py:8
  269.4 175.9 %collective-permute-start.2 = (bf16[1,1792,3,128]{3,1,2,0:T(8,128)(2,1)}, bf16[1,1792,3,128]{3,1,2,0:T(8,128)(2,1)}, u32[]{:S(2)}, u32[]{:S(2)}) collective-permute-start(bf16[1,1792,3,128]{3,1,2,0:T(8,128)(2,1)} %param.14), channel_id=1, source_target_pairs={{0,8},{1,9},{2,10},{3,11},{4,12},{5,13},{6,14},{7,15},{8,0},{9,1},... | collective-permute-start | bytes 4128776 | tf_op jit(solution)/shard_map/ppermute | solution.py:8
  387.3 57.9 %copy-start.4 = (bf16[1792,3,128]{2,0,1:T(8,128)(2,1)S(1)}, bf16[1792,3,128]{2,0,1:T(8,128)(2,1)}, u32[]{:S(2)}) copy-start(bf16[1792,3,128]{2,0,1:T(8,128)(2,1)} %reduce-scatter.2.cloned.1.call-done) | copy-start | bytes 4128772
  445.3 4.8 %copy-start.1 = (bf16[32,3584]{1,0:T(8,128)(2,1)S(1)}, bf16[32,3584]{1,0:T(8,128)(2,1)}, u32[]{:S(2)}) copy-start(bf16[32,3584]{1,0:T(8,128)(2,1)} %param.9) | copy-start | bytes 688132
Sparse Core Ops, SparseCore 0:
  202.4 11.3 all-gather.1
  236.9 17.5 reduce-scatter.1
where the time goes:
time: 458 us; the launch traced here: 457 us
  waiting for transfers between devices  306 us (67%)
  starting transfers between devices  53.7 us (12%)
  local copies, waits for them, and re-layouts  41.5 us (9%)
  other arithmetic  25.7 us (6%)
  matrix products  15.3 us (3%)
  between operations  15 us (3%)
    ppermute x3, waiting for transfers between devices, from_partner(): lax.ppermute(value, axis, [(i, i ^ 1 << bit) for i in range(lax.axis_size...  107 us
    all_to_all x1, waiting for transfers between devices, on_device(): lax.all_to_all(row_grad.reshape(axis_width, slot_cap, model_width), 'expe...  105 us
    all_to_all x1, waiting for transfers between devices, on_device(): lax.all_to_all(send_grads, 'expert', split_axis=0, concat_axis=0, tiled=T...  80.3 us
    all_to_all x1, starting transfers between devices, on_device(): lax.all_to_all(send_rows, 'expert', split_axis=0, concat_axis=0, tiled=True)  14.8 us
    all_to_all x1, starting transfers between devices, on_device(): lax.all_to_all(gate_rows.reshape(axis_width, slot_cap), 'expert', split_a...  12.8 us
  transfers between devices with their start and end apart: 10, of which 8 were waited for; matrix products, arithmetic and copies ran while one was open for 12% of the time, Pallas kernels for 0%

commit v1 on v0

--- a/solution.py
+++ b/solution.py
@@ -2,6 +2,29 @@
 import jax.numpy as jnp
 from jax import lax
 from jax.sharding import PartitionSpec as P
+
+
+def in_blocks(x, dim, size):
+    before, after = (x.shape[:dim], x.shape[dim + 1 :])
+    return jnp.moveaxis(x.reshape(*before, size, -1, *after), dim, 0)
+
+
+def joined_along(tiles, dim):
+    shape = list(tiles.shape[1:])
+    shape[dim] *= tiles.shape[0]
+    return jnp.moveaxis(tiles, 0, dim).reshape(shape)
+
+
+def rotated_exchange(shard, axis, split_dim, concat_dim):
+    peers, index = (lax.axis_size(axis), lax.axis_index(axis))
+    tiles = in_blocks(shard, split_dim, peers)
+    out = tiles
+    for lap in range(1, peers):
+        target, source = ((index + lap) % peers, (index - lap) % peers)
+        sent = lax.dynamic_index_in_dim(tiles, target, 0)
+        other = lax.ppermute(sent, axis, [(i, (i + lap) % peers) for i in range(peers)])
+        out = lax.dynamic_update_slice_in_dim(out, other, source, axis=0)
+    return joined_along(out, concat_dim)
 
 
 def from_partner(value, axis, bit):
@@ -61,7 +84,7 @@
         .reshape(axis_width, slot_cap)
     )
     recv_rows, recv_grads, recv_gate = (
-        lax.all_to_all(send_rows, "expert", split_axis=0, concat_axis=0, tiled=True),
+        rotated_exchange(send_rows, "expert", 0, 0),
         lax.all_to_all(send_grads, "expert", split_axis=0, concat_axis=0, tiled=True),
         lax.all_to_all(send_gate, "expert", split_axis=0, concat_axis=0, tiled=True),
     )

time: 458 us -> 468 us (1.022)
  waiting for transfers between devices: 306 us -> 272 us
  starting transfers between devices: 53.7 us -> 82.7 us
  local copies, waits for them, and re-layouts: 41.5 us -> 54 us
    all_to_all x1, waiting for transfers between devices: 80.3 us -> 0.01 us  [on_device(): lax.all_to_all(send_grads, 'expert', split_axis=0, concat_axis=0, tiled=T...]
    ppermute x0 -> x15, waiting for transfers between devices: none -> 62 us  [rotated_exchange(): lax.ppermute(sent, axis, [(i, (i + lap) % peers) for i in range(peers)])]
    ppermute x0 -> x15, starting transfers between devices: none -> 56 us  [rotated_exchange(): lax.ppermute(sent, axis, [(i, (i + lap) % peers) for i in range(peers)])]
    ppermute x3, waiting for transfers between devices: 107 us -> 54.5 us  [from_partner(): lax.ppermute(value, axis, [(i, i ^ 1 << bit) for i in range(lax.axis_size...]
    all_to_all x1, waiting for transfers between devices: 0.01 us -> 46.7 us  [on_device(): lax.all_to_all(send_gate, 'expert', split_axis=0, concat_axis=0, tiled=True)]
    all_to_all x1 -> x0, starting transfers between devices: 14.8 us -> none  [on_device(): lax.all_to_all(send_rows, 'expert', split_axis=0, concat_axis=0, tiled=True)]
    dynamic_update_slice x0 -> x14, local copies, waits for them, and re-layouts: none -> 9.52 us  [rotated_exchange(): out = lax.dynamic_update_slice_in_dim(out, other, source, axis=0)]
    all_gather x1, waiting for transfers between devices: 6.04 us -> 0.07 us  [on_device(): whole = lax.all_gather(weights, 'dp', axis=1, tiled=True)[0]]
  transfers between devices with their start and end apart: 10 -> 24, of which waited for: 8 -> 9; matrix products, arithmetic and copies ran while one was open for 12% -> 12% of each run, Pallas kernels for 0% -> 0%
where the time goes in v1:
time: 468 us; the launch traced here: 466 us
  waiting for transfers between devices  272 us (58%)
  starting transfers between devices  82.7 us (18%)
  local copies, waits for them, and re-layouts  54 us (12%)
  other arithmetic  26.3 us (6%)
  matrix products  16 us (3%)
  between operations  15.1 us (3%)
    all_to_all x1, waiting for transfers between devices, on_device(): lax.all_to_all(row_grad.reshape(axis_width, slot_cap, model_width), 'expe...  106 us
    ppermute x15, waiting for transfers between devices, rotated_exchange(): lax.ppermute(sent, axis, [(i, (i + lap) % peers) for i in range(peers)])  62 us
    ppermute x15, starting transfers between devices, rotated_exchange(): lax.ppermute(sent, axis, [(i, (i + lap) % peers) for i in range(peers)])  56 us
    ppermute x3, waiting for transfers between devices, from_partner(): lax.ppermute(value, axis, [(i, i ^ 1 << bit) for i in range(lax.axis_size...  54.5 us
    all_to_all x1, waiting for transfers between devices, on_device(): lax.all_to_all(send_gate, 'expert', split_axis=0, concat_axis=0, tiled=True)  46.7 us
    dynamic_update_slice x14, local copies, waits for them, and re-layouts, rotated_exchange(): out = lax.dynamic_update_slice_in_dim(out, other, source, axis=0)  9.52 us
  transfers between devices with their start and end apart: 24, of which 9 were waited for; matrix products, arithmetic and copies ran while one was open for 12% of the time, Pallas kernels for 0%

profile of v1, /device:TPU:0, one launch (start us, length us, event | category | flops | bytes accessed | tf_op | source)
XLA Modules:
  0.0 466.5 jit_solution(7868042974689385233)
XLA Ops:
  10.2 3.7 gather_fusion.2
  19.4 3.0 collective-permute-start.1
  28.2 4.6 all-to-all-start
  32.8 3.7 gather_fusion.1
  46.8 46.7 %all-to-all-done = bf16[16,1,20]{2,1,0:T(2,128)(2,1)S(1)} async-done(((bf16[16,1,20]{2,1,0:T(2,128)(2,1)}), bf16[16,1,20]{2,1,0:T(2,128)(2,1)S(1)}, u32[]{:S(2)}, u32[]{:S(2)}) %all-to-all-start) | async-done | bytes 672 | tf_op jit(solution)/shard_map/all_to_all | solution.py:89
  93.5 4.5 all-to-all-start.1
  106.0 46.4 %collective-permute-done.3 = bf16[1,1,20,3584]{3,2,0,1:T(8,128)(2,1)S(1)} collective-permute-done((bf16[1,1,20,3584]{3,2,0,1:T(8,128)(2,1)S(1)}, bf16[1,1,20,3584]{3,2,0,1:T(8,128)(2,1)S(1)}, u32[]{:S(2)}, u32[]{:S(2)}) %collective-permute-start.3) | collective-permute-done | bytes 143392 | tf_op jit(solution)/shard_map/ppermute | solution.py:25
  152.4 21.8 %collective-permute-start.7 = (bf16[1,1,20,3584]{3,2,0,1:T(8,128)(2,1)S(1)}, bf16[1,1,20,3584]{3,2,0,1:T(8,128)(2,1)S(1)}, u32[]{:S(2)}, u32[]{:S(2)}) collective-permute-start(bf16[1,1,20,3584]{3,2,0,1:T(8,128)(2,1)S(1)} %get-tuple-element.42), channel_id=1, source_target_pairs={{0,7},{1,8},{2,9},{3,10},{4,11},{5,12},{6,13},{7,14},{8,15},{9,0},... | collective-permute-start | bytes 430088 | tf_op jit(solution)/shard_map/ppermute | solution.py:25
  175.5 12.7 %collective-permute-done.5 = bf16[1,1,20,3584]{3,2,0,1:T(8,128)(2,1)S(1)} collective-permute-done((bf16[1,1,20,3584]{3,2,0,1:T(8,128)(2,1)S(1)}, bf16[1,1,20,3584]{3,2,0,1:T(8,128)(2,1)S(1)}, u32[]{:S(2)}, u32[]{:S(2)}) %collective-permute-start.5) | collective-permute-done | bytes 143392 | tf_op jit(solution)/shard_map/ppermute | solution.py:25
  192.4 3.5 collective-permute-start.11
  196.6 10.1 %collective-permute-start.12 = (bf16[1,1,20,3584]{3,2,0,1:T(8,128)(2,1)S(1)}, bf16[1,1,20,3584]{3,2,0,1:T(8,128)(2,1)S(1)}, u32[]{:S(2)}, u32[]{:S(2)}) collective-permute-start(bf16[1,1,20,3584]{3,2,0,1:T(8,128)(2,1)S(1)} %get-tuple-element.37), channel_id=1, source_target_pairs={{0,12},{1,13},{2,14},{3,15},{4,0},{5,1},{6,2},{7,3},{8,4},{9,5},{1... | collective-permute-start | bytes 430088 | tf_op jit(solution)/shard_map/ppermute | solution.py:25
  210.1 6.2 %collective-permute-start.14 = (bf16[1,1,20,3584]{3,2,0,1:T(8,128)(2,1)S(1)}, bf16[1,1,20,3584]{3,2,0,1:T(8,128)(2,1)S(1)}, u32[]{:S(2)}, u32[]{:S(2)}) collective-permute-start(bf16[1,1,20,3584]{3,2,0,1:T(8,128)(2,1)S(1)} %get-tuple-element.35), channel_id=1, source_target_pairs={{0,14},{1,15},{2,0},{3,1},{4,2},{5,3},{6,4},{7,5},{8,6},{9,7},{10,... | collective-permute-start | bytes 430088 | tf_op jit(solution)/shard_map/ppermute | solution.py:25
  228.5 4.1 multiply_convert_fusion
  232.6 4.1 convert_element_type.114
  256.7 7.2 %all-to-all-start.3 = ((bf16[16,1,20]{2,1,0:T(2,128)(2,1)}), bf16[16,1,20]{2,1,0:T(2,128)(2,1)S(1)}, u32[]{:S(2)}, u32[]{:S(2)}) async-start(bf16[16,1,20]{2,1,0:T(2,128)(2,1)} %convert_element_type.138), calls=%async_computation.3 | async-start | bytes 16384 | tf_op jit(solution)/shard_map/all_to_all | solution.py:123
  268.1 3.0 all-to-all-done.3
  271.1 4.7 %all-to-all-start.2 = ((bf16[16,20,3584]{2,1,0:T(8,128)(2,1)}), bf16[16,20,3584]{2,1,0:T(8,128)(2,1)}, u32[]{:S(2)}, u32[]{:S(2)}) async-start(bf16[16,20,3584]{2,1,0:T(8,128)(2,1)} %reshape.351), calls=%async_computation.2 | async-start | bytes 5505024 | tf_op jit(solution)/shard_map/all_to_all | solution.py:116
  281.8 106.0 %all-to-all-done.2 = bf16[16,20,3584]{2,1,0:T(8,128)(2,1)} async-done(((bf16[16,20,3584]{2,1,0:T(8,128)(2,1)}), bf16[16,20,3584]{2,1,0:T(8,128)(2,1)}, u32[]{:S(2)}, u32[]{:S(2)}) %all-to-all-start.2) | async-done | bytes 2293792 | tf_op jit(solution)/shard_map/all_to_all | solution.py:116
  390.5 2.9 gather_fusion.3
  393.5 3.6 fusion.3
  397.1 3.2 fusion.5
  400.3 26.1 %collective-permute-done.16 = bf16[1,1792,3,128]{3,1,2,0:T(8,128)(2,1)} collective-permute-done((bf16[1,1792,3,128]{3,1,2,0:T(8,128)(2,1)}, bf16[1,1792,3,128]{3,1,2,0:T(8,128)(2,1)}, u32[]{:S(2)}, u32[]{:S(2)}) %collective-permute-start.16) | collective-permute-done | bytes 1376288 | tf_op jit(solution)/shard_map/ppermute | solution.py:31
  426.4 28.4 %collective-permute-done.17 = bf16[1,1792,3,128]{3,1,2,0:T(8,128)(2,1)} collective-permute-done((bf16[1,1792,3,128]{3,1,2,0:T(8,128)(2,1)}, bf16[1,1792,3,128]{3,1,2,0:T(8,128)(2,1)}, u32[]{:S(2)}, u32[]{:S(2)}) %collective-permute-start.17) | collective-permute-done | bytes 1376288 | tf_op jit(solution)/shard_map/ppermute | solution.py:31
  454.9 4.8 %fusion.8 = (bf16[1,1792,3,128]{3,1,2,0:T(8,128)(2,1)}, bf16[1,1792,3,128]{3,1,2,0:T(8,128)(2,1)}) fusion(bf16[1792,3,128]{2,0,1:T(8,128)(2,1)S(1)} %copy-done.3, bf16[1,1792,3,128]{3,1,2,0:T(8,128)(2,1)} %collective-permute-done.17, bf16[1,1792,3,128]{3,1,2,0:T(8,128)(2,1)} %param.14, pred[]{:T(512)S(6)} %eq.130, ...), kind=kLoop, calls=%fused_computation.23 | loop fusion | flops 10321920 | bytes 9633793 | tf_op jit(solution)/shard_map/convert_element_type | solution.py:145
  (120 shorter events, 86.2 us)
Async XLA Ops:
  19.4 21.6 %collective-permute-start.1 = (bf16[1,1,20,3584]{3,2,0,1:T(8,128)(2,1)S(1)}, bf16[1,1,20,3584]{3,2,0,1:T(8,128)(2,1)S(1)}, u32[]{:S(2)}, u32[]{:S(2)}) collective-permute-start(bf16[1,1,20,3584]{3,2,0,1:T(8,128)(2,1)S(1)} %constant_dynamic-slice_fusion.14), channel_id=1, source_target_pairs={{0,1},{1,2},{2,3},{3,4},{4,5},{5,6},{6,7},{7,8},{8,9},{9,10},{10,1... | collective-permute-start | bytes 430088 | tf_op jit(solution)/shard_map/ppermute | solution.py:25
  22.4 185.0 %collective-permute-start = (bf16[1,1792,3,128]{3,1,2,0:T(8,128)(2,1)}, bf16[1,1792,3,128]{3,1,2,0:T(8,128)(2,1)}, u32[]{:S(2)}, u32[]{:S(2)}) collective-permute-start(bf16[1,1792,3,128]{3,1,2,0:T(8,128)(2,1)} %param.12), channel_id=1, source_target_pairs={{0,8},{1,9},{2,10},{3,11},{4,12},{5,13},{6,14},{7,15},{8,0},{9,1},... | collective-permute-start | bytes 4128776 | tf_op jit(solution)/shard_map/ppermute | solution.py:31
  28.2 65.3 %all-to-all-start = ((bf16[16,1,20]{2,1,0:T(2,128)(2,1)}), bf16[16,1,20]{2,1,0:T(2,128)(2,1)S(1)}, u32[]{:S(2)}, u32[]{:S(2)}) async-start(bf16[16,1,20]{2,1,0:T(2,128)(2,1)} %convert_element_type.137), calls=%async_computation | async-start | bytes 16384 | tf_op jit(solution)/shard_map/all_to_all | solution.py:89
  43.5 60.4 %collective-permute-start.2 = (bf16[1,1,20,3584]{3,2,0,1:T(8,128)(2,1)S(1)}, bf16[1,1,20,3584]{3,2,0,1:T(8,128)(2,1)S(1)}, u32[]{:S(2)}, u32[]{:S(2)}) collective-permute-start(bf16[1,1,20,3584]{3,2,0,1:T(8,128)(2,1)S(1)} %get-tuple-element.47), channel_id=1, source_target_pairs={{0,2},{1,3},{2,4},{3,5},{4,6},{5,7},{6,8},{7,9},{8,10},{9,11},{10,... | collective-permute-start | bytes 430088 | tf_op jit(solution)/shard_map/ppermute | solution.py:25
  93.5 134.9 %all-to-all-start.1 = ((bf16[16,20,3584]{2,1,0:T(8,128)(2,1)}), bf16[16,20,3584]{2,1,0:T(8,128)(2,1)}, u32[]{:S(2)}, u32[]{:S(2)}) async-start(bf16[16,20,3584]{2,1,0:T(8,128)(2,1)} %broadcast_select_fusion.1), calls=%async_computation.1 | async-start | bytes 5505024 | tf_op jit(solution)/shard_map/all_to_all | solution.py:88
  98.0 128.5 %all-gather.2.cloned.1.call-start = ((), (), s32[]{:S(2)}) async-start(), calls=%async_computation.5 | async-start | bytes 4128768 | tf_op jit(solution)/shard_map/all_gather | solution.py:91
  98.2 54.2 %collective-permute-start.3 = (bf16[1,1,20,3584]{3,2,0,1:T(8,128)(2,1)S(1)}, bf16[1,1,20,3584]{3,2,0,1:T(8,128)(2,1)S(1)}, u32[]{:S(2)}, u32[]{:S(2)}) collective-permute-start(bf16[1,1,20,3584]{3,2,0,1:T(8,128)(2,1)S(1)} %get-tuple-element.46), channel_id=1, source_target_pairs={{0,3},{1,4},{2,5},{3,6},{4,7},{5,8},{6,9},{7,10},{8,11},{9,12},{10... | collective-permute-start | bytes 430088 | tf_op jit(solution)/shard_map/ppermute | solution.py:25
  100.9 74.0 %collective-permute-start.4 = (bf16[1,1,20,3584]{3,2,0,1:T(8,128)(2,1)S(1)}, bf16[1,1,20,3584]{3,2,0,1:T(8,128)(2,1)S(1)}, u32[]{:S(2)}, u32[]{:S(2)}) collective-permute-start(bf16[1,1,20,3584]{3,2,0,1:T(8,128)(2,1)S(1)} %get-tuple-element.45), channel_id=1, source_target_pairs={{0,4},{1,5},{2,6},{3,7},{4,8},{5,9},{6,10},{7,11},{8,12},{9,13},{1... | collective-permute-start | bytes 430088 | tf_op jit(solution)/shard_map/ppermute | solution.py:25
  102.4 85.9 %collective-permute-start.5 = (bf16[1,1,20,3584]{3,2,0,1:T(8,128)(2,1)S(1)}, bf16[1,1,20,3584]{3,2,0,1:T(8,128)(2,1)S(1)}, u32[]{:S(2)}, u32[]{:S(2)}) collective-permute-start(bf16[1,1,20,3584]{3,2,0,1:T(8,128)(2,1)S(1)} %get-tuple-element.44), channel_id=1, source_target_pairs={{0,5},{1,6},{2,7},{3,8},{4,9},{5,10},{6,11},{7,12},{8,13},{9,14},{... | collective-permute-start | bytes 430088 | tf_op jit(solution)/shard_map/ppermute | solution.py:25
  103.9 87.8 %collective-permute-start.6 = (bf16[1,1,20,3584]{3,2,0,1:T(8,128)(2,1)S(1)}, bf16[1,1,20,3584]{3,2,0,1:T(8,128)(2,1)S(1)}, u32[]{:S(2)}, u32[]{:S(2)}) collective-permute-start(bf16[1,1,20,3584]{3,2,0,1:T(8,128)(2,1)S(1)} %get-tuple-element.43), channel_id=1, source_target_pairs={{0,6},{1,7},{2,8},{3,9},{4,10},{5,11},{6,12},{7,13},{8,14},{9,15},... | collective-permute-start | bytes 430088 | tf_op jit(solution)/shard_map/ppermute | solution.py:25
  152.4 40.0 %collective-permute-start.7 = (bf16[1,1,20,3584]{3,2,0,1:T(8,128)(2,1)S(1)}, bf16[1,1,20,3584]{3,2,0,1:T(8,128)(2,1)S(1)}, u32[]{:S(2)}, u32[]{:S(2)}) collective-permute-start(bf16[1,1,20,3584]{3,2,0,1:T(8,128)(2,1)S(1)} %get-tuple-element.42), channel_id=1, source_target_pairs={{0,7},{1,8},{2,9},{3,10},{4,11},{5,12},{6,13},{7,14},{8,15},{9,0},... | collective-permute-start | bytes 430088 | tf_op jit(solution)/shard_map/ppermute | solution.py:25
  174.9 21.8 %collective-permute-start.8 = (bf16[1,1,20,3584]{3,2,0,1:T(8,128)(2,1)S(1)}, bf16[1,1,20,3584]{3,2,0,1:T(8,128)(2,1)S(1)}, u32[]{:S(2)}, u32[]{:S(2)}) collective-permute-start(bf16[1,1,20,3584]{3,2,0,1:T(8,128)(2,1)S(1)} %get-tuple-element.41), channel_id=1, source_target_pairs={{0,8},{1,9},{2,10},{3,11},{4,12},{5,13},{6,14},{7,15},{8,0},{9,1},... | collective-permute-start | bytes 430088 | tf_op jit(solution)/shard_map/ppermute | solution.py:25
  188.3 21.8 %collective-permute-start.9 = (bf16[1,1,20,3584]{3,2,0,1:T(8,128)(2,1)S(1)}, bf16[1,1,20,3584]{3,2,0,1:T(8,128)(2,1)S(1)}, u32[]{:S(2)}, u32[]{:S(2)}) collective-permute-start(bf16[1,1,20,3584]{3,2,0,1:T(8,128)(2,1)S(1)} %get-tuple-element.40), channel_id=1, source_target_pairs={{0,9},{1,10},{2,11},{3,12},{4,13},{5,14},{6,15},{7,0},{8,1},{9,2},... | collective-permute-start | bytes 430088 | tf_op jit(solution)/shard_map/ppermute | solution.py:25
  191.7 25.2 %collective-permute-start.10 = (bf16[1,1,20,3584]{3,2,0,1:T(8,128)(2,1)S(1)}, bf16[1,1,20,3584]{3,2,0,1:T(8,128)(2,1)S(1)}, u32[]{:S(2)}, u32[]{:S(2)}) collective-permute-start(bf16[1,1,20,3584]{3,2,0,1:T(8,128)(2,1)S(1)} %get-tuple-element.39), channel_id=1, source_target_pairs={{0,10},{1,11},{2,12},{3,13},{4,14},{5,15},{6,0},{7,1},{8,2},{9,3},... | collective-permute-start | bytes 430088 | tf_op jit(solution)/shard_map/ppermute | solution.py:25
  192.4 27.6 %collective-permute-start.11 = (bf16[1,1,20,3584]{3,2,0,1:T(8,128)(2,1)S(1)}, bf16[1,1,20,3584]{3,2,0,1:T(8,128)(2,1)S(1)}, u32[]{:S(2)}, u32[]{:S(2)}) collective-permute-start(bf16[1,1,20,3584]{3,2,0,1:T(8,128)(2,1)S(1)} %get-tuple-element.38), channel_id=1, source_target_pairs={{0,11},{1,12},{2,13},{3,14},{4,15},{5,0},{6,1},{7,2},{8,3},{9,4},{... | collective-permute-start | bytes 430088 | tf_op jit(solution)/shard_map/ppermute | solution.py:25
  196.6 24.1 %collective-permute-start.12 = (bf16[1,1,20,3584]{3,2,0,1:T(8,128)(2,1)S(1)}, bf16[1,1,20,3584]{3,2,0,1:T(8,128)(2,1)S(1)}, u32[]{:S(2)}, u32[]{:S(2)}) collective-permute-start(bf16[1,1,20,3584]{3,2,0,1:T(8,128)(2,1)S(1)} %get-tuple-element.37), channel_id=1, source_target_pairs={{0,12},{1,13},{2,14},{3,15},{4,0},{5,1},{6,2},{7,3},{8,4},{9,5},{1... | collective-permute-start | bytes 430088 | tf_op jit(solution)/shard_map/ppermute | solution.py:25
  207.4 14.1 %collective-permute-start.13 = (bf16[1,1,20,3584]{3,2,0,1:T(8,128)(2,1)S(1)}, bf16[1,1,20,3584]{3,2,0,1:T(8,128)(2,1)S(1)}, u32[]{:S(2)}, u32[]{:S(2)}) collective-permute-start(bf16[1,1,20,3584]{3,2,0,1:T(8,128)(2,1)S(1)} %get-tuple-element.36), channel_id=1, source_target_pairs={{0,13},{1,14},{2,15},{3,0},{4,1},{5,2},{6,3},{7,4},{8,5},{9,6},{10... | collective-permute-start | bytes 430088 | tf_op jit(solution)/shard_map/ppermute | solution.py:25
  210.0 187.1 %reduce-scatter.2.cloned.1.call-start = ((), (), s32[]{:S(2)}) async-start(), calls=%async_computation.6 | async-start | bytes 4128768 | tf_op jit(solution)/shard_map/reduce_scatter | solution.py:137
  210.1 12.1 %collective-permute-start.14 = (bf16[1,1,20,3584]{3,2,0,1:T(8,128)(2,1)S(1)}, bf16[1,1,20,3584]{3,2,0,1:T(8,128)(2,1)S(1)}, u32[]{:S(2)}, u32[]{:S(2)}) collective-permute-start(bf16[1,1,20,3584]{3,2,0,1:T(8,128)(2,1)S(1)} %get-tuple-element.35), channel_id=1, source_target_pairs={{0,14},{1,15},{2,0},{3,1},{4,2},{5,3},{6,4},{7,5},{8,6},{9,7},{10,... | collective-permute-start | bytes 430088 | tf_op jit(solution)/shard_map/ppermute | solution.py:25
  216.9 5.9 %collective-permute-start.15 = (bf16[1,1,20,3584]{3,2,0,1:T(8,128)(2,1)S(1)}, bf16[1,1,20,3584]{3,2,0,1:T(8,128)(2,1)S(1)}, u32[]{:S(2)}, u32[]{:S(2)}) collective-permute-start(bf16[1,1,20,3584]{3,2,0,1:T(8,128)(2,1)S(1)} %get-tuple-element.34), channel_id=1, source_target_pairs={{0,15},{1,0},{2,1},{3,2},{4,3},{5,4},{6,5},{7,6},{8,7},{9,8},{10,9... | collective-permute-start | bytes 430088 | tf_op jit(solution)/shard_map/ppermute | solution.py:25
  256.7 14.4 %all-to-all-start.3 = ((bf16[16,1,20]{2,1,0:T(2,128)(2,1)}), bf16[16,1,20]{2,1,0:T(2,128)(2,1)S(1)}, u32[]{:S(2)}, u32[]{:S(2)}) async-start(bf16[16,1,20]{2,1,0:T(2,128)(2,1)} %convert_element_type.138), calls=%async_computation.3 | async-start | bytes 16384 | tf_op jit(solution)/shard_map/all_to_all | solution.py:123
  271.1 116.7 %all-to-all-start.2 = ((bf16[16,20,3584]{2,1,0:T(8,128)(2,1)}), bf16[16,20,3584]{2,1,0:T(8,128)(2,1)}, u32[]{:S(2)}, u32[]{:S(2)}) async-start(bf16[16,20,3584]{2,1,0:T(8,128)(2,1)} %reshape.351), calls=%async_computation.2 | async-start | bytes 5505024 | tf_op jit(solution)/shard_map/all_to_all | solution.py:116
  275.8 150.6 %collective-permute-start.16 = (bf16[1,1792,3,128]{3,1,2,0:T(8,128)(2,1)}, bf16[1,1792,3,128]{3,1,2,0:T(8,128)(2,1)}, u32[]{:S(2)}, u32[]{:S(2)}) collective-permute-start(bf16[1,1792,3,128]{3,1,2,0:T(8,128)(2,1)} %param.13), channel_id=1, source_target_pairs={{0,8},{1,9},{2,10},{3,11},{4,12},{5,13},{6,14},{7,15},{8,0},{9,1},... | collective-permute-start | bytes 4128776 | tf_op jit(solution)/shard_map/ppermute | solution.py:31
  278.4 176.5 %collective-permute-start.17 = (bf16[1,1792,3,128]{3,1,2,0:T(8,128)(2,1)}, bf16[1,1792,3,128]{3,1,2,0:T(8,128)(2,1)}, u32[]{:S(2)}, u32[]{:S(2)}) collective-permute-start(bf16[1,1792,3,128]{3,1,2,0:T(8,128)(2,1)} %param.14), channel_id=1, source_target_pairs={{0,8},{1,9},{2,10},{3,11},{4,12},{5,13},{6,14},{7,15},{8,0},{9,1},... | collective-permute-start | bytes 4128776 | tf_op jit(solution)/shard_map/ppermute | solution.py:31
  (8 other events, 157.0 us)
Sparse Core Ops, SparseCore 0:
  210.1 16.3 all-gather.1
  251.6 11.9 reduce-scatter.1
